TPU v7x, 512 devices: a whole 4x8x8 slice. The times are simulated.
512 devices in a mesh: blk: 16 (over x_lo, y), exp: 32 (over z, x_hi, core).
Axes of the slice: x: 4 (x_hi: 2, x_lo: 2; x = x_hi * 2 + x_lo), y: 8, z: 8, core: 2. Of those that a mesh axis runs over, the one named last changes fastest.
Arguments:
- residual: bfloat16 [32, 2048, 1024], P('exp', 'blk'), may hold values from -6 to 6
- queries: bfloat16 [32, 2048, 1024], P('exp', 'blk'), may hold values from -6 to 6
- suffix_kv: bfloat16 [32, 2048, 1024], P('exp', 'blk'), may hold values from -6 to 6
- prompt_kv: bfloat16 [32, 1024, 1024], P('exp', 'blk'), may hold values from -6 to 6
- prompt_lengths: int32 [32], P('exp'), may hold values from 1 to 1024, as said below
- block_keep: int32 [32, 32], P('exp', 'blk'), may hold values 0 or 1
- suffix_lengths: int32 [32, 16, 4], P('exp', 'blk'), may hold values from 1 to 64, 128 in all within a row
- out_weight: bfloat16 [1024, 1024], P('exp'), may hold values from -0.75 to 0.75
- routes: int32 [32, 2048, 8], P('exp', 'blk'), may hold values from 0 to 31, all different within a row; in each aligned block of 128 rows (0 to 127, 128 to 255, ..., all dimensions but the last counted through in order) at most 40 rows name the same one
- route_weight: float32 [32, 2048, 8], P('exp', 'blk'), may hold values from 0.02 to 0.25
- gate_up_weight: bfloat16 [32, 1024, 1024], P('exp'), may hold values from -0.1875 to 0.1875
- down_weight: bfloat16 [32, 512, 1024], P('exp'), may hold values from -0.25 to 0.25
- page_owner: int32 [32, 128, 1], P('exp', 'blk'), may hold values from 0 to 15; in each aligned block of 8 rows (0 to 7, 8 to 15, ..., all dimensions but the last counted through in order) at most 2 rows name the same one
Outputs:
- attended: bfloat16 [32, 2048, 1024], P('exp', 'blk')
- layer_out: bfloat16 [32, 2048, 1024], P('exp', 'blk')
- cache_pages: bfloat16 [32, 4096, 1024], P('exp', 'blk')
Inputs may be any that keep to these rules, and one draw needn't show every extreme that they name: `prompt_lengths`: some group's prompt length equals 1024. `suffix_lengths`: each device's 4 request lengths sum to 128. `routes`: each token names 8 different experts; among the tokens of one device at most 40 name any one expert, and that bound is reached. `page_owner`: among the 8 pages of one device at most 2 go to any one owner, and that bound is reached.
All inputs are finite; a program needn't handle non-finite values. No bound on the sum of `block_keep` on one device may be relied on, other than what follows from the above.
Results may differ from a plain program's by a relative error of at most 0.013.
Values may be sent and summed in bfloat16 or wider, within the bound.
No kernel may reach another device: no remote copies, remote signals or barrier semaphores. Data moves between devices by JAX's collectives and lax.ppermute only.
A program may use at most 64 MiB of HBM per device.

v0:
```python
import jax
import jax.numpy as jnp
from jax import lax
from jax.sharding import PartitionSpec as P

D = 1024
H = 16
KVH = 8
HD = 64
FF = 512
TOPK = 8
EXP_DEV = 1
KB = 32
PAGE = 8
SCALE = 0.125
NEGATIVE = -1e30
EPSILON = 1e-06


def segment_of(lengths, count):
    ends = jnp.cumsum(lengths)
    position = jnp.arange(count, dtype=jnp.int32)
    return jnp.sum((position[:, None] >= ends[None, :]).astype(jnp.int32), axis=1)


def rank_within(labels, count):
    onehot = (labels[:, None] == jnp.arange(count, dtype=jnp.int32)[None, :]).astype(jnp.int32)
    before = jnp.cumsum(onehot, axis=0) - onehot
    return jnp.sum(before * onehot, axis=1)


def absorb(carry_state, query_heads, key_heads, value_heads, visible):
    running_max, denom, numerator = carry_state
    scores = (
        jnp.einsum("tkgd,skd->tkgs", query_heads, key_heads, preferred_element_type=jnp.float32)
        * SCALE
    )
    new_max = jnp.maximum(running_max, jnp.max(jnp.where(visible, scores, NEGATIVE), axis=-1))
    factor = jnp.exp(running_max - new_max)
    weight = jnp.where(visible, jnp.exp(scores - new_max[..., None]), 0.0)
    denom = denom * factor + jnp.sum(weight, axis=-1)
    added = jnp.einsum(
        "tkgs,skd->tkgd",
        weight.astype(jnp.bfloat16),
        value_heads,
        preferred_element_type=jnp.float32,
    )
    numerator = numerator * factor[..., None] + added
    return (new_max, denom, numerator)


def local(
    residual,
    queries,
    suffix_kv,
    prompt_kv,
    prompt_lengths,
    block_keep,
    suffix_lengths,
    out_weight,
    routes,
    route_weight,
    gate_up_weight,
    down_weight,
    page_owner,
):
    tok_rows = queries.shape[1]
    kv_width = suffix_kv.shape[2] // 2
    group_size = H // KVH
    query_heads = queries[0].reshape(tok_rows, KVH, group_size, HD)
    own_keys = suffix_kv[0, :, :kv_width].reshape(tok_rows, KVH, HD)
    own_values = suffix_kv[0, :, kv_width:].reshape(tok_rows, KVH, HD)
    segment = segment_of(suffix_lengths[0, 0], tok_rows)
    position = jnp.arange(tok_rows, dtype=jnp.int32)
    own_seen = ((segment[:, None] == segment[None, :]) & (position[None, :] <= position[:, None]))[
        :, None, None, :
    ]
    start_state = (
        jnp.full((tok_rows, KVH, group_size), NEGATIVE, jnp.float32),
        jnp.zeros((tok_rows, KVH, group_size), jnp.float32),
        jnp.zeros((tok_rows, KVH, group_size, HD), jnp.float32),
    )
    carry_state = absorb(start_state, query_heads, own_keys, own_values, own_seen)
    block_rows = prompt_kv.shape[1]
    keep_rows = jnp.repeat(block_keep[0], KB)
    position_abs = lax.axis_index("blk") * block_rows + jnp.arange(block_rows, dtype=jnp.int32)
    live_keys = ((keep_rows > 0) & (position_abs < prompt_lengths[0])).astype(jnp.int32)[None, :]
    piece_kv = lax.all_gather(prompt_kv, "blk", axis=1, tiled=True)
    piece_live = lax.all_gather(live_keys, "blk", axis=1, tiled=True)
    count = piece_kv.shape[1]
    key_heads = piece_kv[0, :, :kv_width].reshape(count, KVH, HD)
    value_heads = piece_kv[0, :, kv_width:].reshape(count, KVH, HD)
    visible = (piece_live[0] > 0)[None, None, None, :]
    running_max, denom, numerator = absorb(
        carry_state, query_heads, key_heads, value_heads, visible
    )
    attended = (numerator / denom[..., None]).reshape(tok_rows, H * HD).astype(jnp.bfloat16)
    projected = jnp.dot(
        attended,
        lax.all_gather(out_weight, "exp", axis=0, tiled=True),
        preferred_element_type=jnp.float32,
    )
    stream = (residual[0].astype(jnp.float32) + projected).astype(jnp.bfloat16)
    stream_f32 = stream.astype(jnp.float32)
    normed = (
        stream_f32 * lax.rsqrt(jnp.mean(stream_f32 * stream_f32, axis=-1, keepdims=True) + EPSILON)
    ).astype(jnp.bfloat16)
    exp_count = lax.axis_size("exp")
    experts = EXP_DEV * exp_count
    capacity = min(tok_rows, 5 * tok_rows * TOPK // (4 * experts))
    flat_routes = routes[0].reshape(-1)
    slot_index = flat_routes * capacity + rank_within(flat_routes, experts)
    dispatch = (
        jnp.zeros((experts * capacity, D), jnp.bfloat16)
        .at[slot_index]
        .set(jnp.repeat(normed, TOPK, axis=0))
    )
    dispatch = dispatch.reshape(experts, capacity, D)
    arrived = lax.all_to_all(dispatch, "exp", split_axis=0, concat_axis=0, tiled=True)
    count = arrived.shape[1]
    grouped = arrived.reshape(exp_count, EXP_DEV, count, D)
    picked_rows = grouped[:, 0].reshape(exp_count * count, D)
    gate_up = jnp.dot(picked_rows, gate_up_weight[0], preferred_element_type=jnp.float32)
    hidden = (jax.nn.silu(gate_up[:, :FF]) * gate_up[:, FF:]).astype(jnp.bfloat16)
    result = jnp.dot(hidden, down_weight[0], preferred_element_type=jnp.float32).astype(
        jnp.bfloat16
    )
    results = [result.reshape(exp_count, count, D)]
    outgoing = jnp.stack(results, axis=1).reshape(exp_count * EXP_DEV, count, D)
    returned = lax.all_to_all(outgoing, "exp", split_axis=0, concat_axis=0, tiled=True)
    picked = (
        returned.reshape(experts * capacity, D)[slot_index]
        .astype(jnp.float32)
        .reshape(tok_rows, TOPK, D)
    )
    layer_out = (stream_f32 + jnp.sum(picked * route_weight[0][:, :, None], axis=1)).astype(
        jnp.bfloat16
    )
    page_count = block_rows // PAGE
    blk_count = lax.axis_size("blk")
    page_capacity = max(2, 2 * page_count // blk_count)
    page_rows = prompt_kv[0].reshape(page_count, PAGE, 2 * kv_width)
    owners = page_owner[0, :, 0]
    page_slot = owners * page_capacity + rank_within(owners, blk_count)
    outgoing_pages = (
        jnp.zeros((blk_count * page_capacity, PAGE, 2 * kv_width), jnp.bfloat16)
        .at[page_slot]
        .set(page_rows)
    )
    arrived_pages = lax.all_to_all(outgoing_pages, "blk", split_axis=0, concat_axis=0, tiled=True)
    cache_pages = arrived_pages.reshape(1, blk_count * page_capacity * PAGE, 2 * kv_width)
    return (attended[None], layer_out[None], cache_pages)


def solution(mesh):
    return jax.shard_map(
        local,
        mesh=mesh,
        in_specs=(
            P("exp", "blk", None),
            P("exp", "blk", None),
            P("exp", "blk", None),
            P("exp", "blk", None),
            P("exp"),
            P("exp", "blk"),
            P("exp", "blk", None),
            P("exp", None),
            P("exp", "blk", None),
            P("exp", "blk", None),
            P("exp", None, None),
            P("exp", None, None),
            P("exp", "blk", None),
        ),
        out_specs=(P("exp", "blk", None), P("exp", "blk", None), P("exp", "blk", None)),
        check_vma=False,
    )
```

profile of v0, /device:TPU:1, one launch (start us, length us, event | category | flops | bytes accessed | tf_op | source)
XLA Modules:
  0.0 363.6 jit_solution(11211758966048198514)
XLA Ops:
  9.4 0.8 copy.48
  11.6 1.0 fusion.51
  12.7 0.8 reduce-window.18
  13.6 9.0 %reduce-window.19 = s32[32,8,128]{2,1,0:T(8,128)S(1)} reduce-window(s32[32,8,128]{2,1,0:T(8,128)S(1)} %fusion.39, s32[]{:T(128)} %constant.17.clone.1), window={size=1x1x128 pad=0_0x0_0x127_0}, to_apply=%region_6.7 | reduce-window | flops 4161536 | bytes 262148 | tf_op jit(solution)/shard_map/reduce-window.1
  23.0 1.3 dynamic-slice
  25.2 1.1 copy.41
  26.8 15.1 %all-reduce = s32[1024]{0:T(1024)S(1)} all-reduce(s32[1024]{0:T(1024)S(1)} %fusion.43), channel_id=1, replica_groups=mesh['blk'=16,'exp'=32] {'blk'}, use_global_device_ids=true, to_apply=%add | all-reduce | flops 1024 | bytes 8192
  43.3 1.9 select_reduce_fusion
  45.2 35.0 %all-gather.3.cloned.1.call-done = bf16[1,1024,1024]{2,1,0:T(8,128)(2,1)} async-done(((bf16[1,64,1024]{2,1,0:T(8,128)(2,1)}), bf16[1,1024,1024]{2,1,0:T(8,128)(2,1)}) %all-gather.3.cloned.1.call-update) | async-done | bytes 2097168 | tf_op jit(solution)/shard_map/all_gather | solution.py:88
  80.2 2.7 fusion.50
  82.9 1.3 copy.45
  84.2 1.5 copy.44
  85.7 2.9 fusion
  89.0 2.2 fusion.3
  91.2 1.5 fusion.17
  93.1 84.1 %all-gather.5.cloned.1.call-done = bf16[1024,1024]{1,0:T(8,128)(2,1)} async-done(((bf16[32,1024]{1,0:T(8,128)(2,1)}), bf16[1024,1024]{1,0:T(8,128)(2,1)}) %all-gather.5.cloned.1.call-update) | async-done | bytes 2097168 | tf_op jit(solution)/shard_map/all_gather | solution.py:100
  177.2 2.1 multiply_reduce_fusion
  179.5 7.1 %scatter_custom_fusion = bf16[1280,1024]{1,0:T(8,128)(2,1)} fusion(s32[1024]{0:T(1024)S(1)} %bitcast.143, bf16[]{:T(256)} %constant.12.clone.1, bf16[128,1024]{1,0:T(8,128)(2,1)S(1)} %multiply_convert_fusion), kind=kCustom, calls=%fused_computation.19 | custom fusion | bytes 2883586 | tf_op jit(solution)/shard_map/scatter | solution.py:116
  186.6 4.8 %all-to-all-start = ((bf16[32,40,1024]{2,1,0:T(8,128)(2,1)}), bf16[32,40,1024]{2,1,0:T(8,128)(2,1)}, u32[]{:S(2)}, u32[]{:S(2)}) async-start(bf16[32,40,1024]{2,1,0:T(8,128)(2,1)} %bitcast.128), calls=%async_computation | async-start | bytes 5242880 | tf_op jit(solution)/shard_map/all_to_all | solution.py:119
  191.7 0.9 broadcast_in_dim.91
  192.5 2.1 scatter_fusion
  194.6 57.8 %all-to-all-done = bf16[32,40,1024]{2,1,0:T(8,128)(2,1)} async-done(((bf16[32,40,1024]{2,1,0:T(8,128)(2,1)}), bf16[32,40,1024]{2,1,0:T(8,128)(2,1)}, u32[]{:S(2)}, u32[]{:S(2)}) %all-to-all-start) | async-done | bytes 2621472 | tf_op jit(solution)/shard_map/all_to_all | solution.py:119
  252.4 7.4 %all-to-all-start.2 = ((bf16[32,8,1024]{2,1,0:T(8,128)(2,1)}), bf16[32,8,1024]{2,1,0:T(8,128)(2,1)S(1)}, u32[]{:S(2)}, u32[]{:S(2)}) async-start(bf16[32,8,1024]{2,1,0:T(8,128)(2,1)} %scatter_fusion), calls=%async_computation.2 | async-start | bytes 1048576 | tf_op jit(solution)/shard_map/all_to_all | solution.py:150
  259.8 4.7 %fusion.10 = f32[1280,1024]{1,0:T(8,128)S(1)} fusion(bf16[1280,1024]{1,0:T(8,128)(2,1)} %bitcast.32, bf16[1,1024,1024]{2,1,0:T(8,128)(2,1)S(1)} %copy-done), kind=kOutput, calls=%fused_computation.17 | convolution fusion | flops 2684354560 | bytes 9961472 | tf_op jit(solution)/shard_map/dot_general | solution.py:123
  264.6 3.1 convolution_convert_fusion
  267.7 5.3 %all-to-all-done.2 = bf16[32,8,1024]{2,1,0:T(8,128)(2,1)S(1)} async-done(((bf16[32,8,1024]{2,1,0:T(8,128)(2,1)}), bf16[32,8,1024]{2,1,0:T(8,128)(2,1)S(1)}, u32[]{:S(2)}, u32[]{:S(2)}) %all-to-all-start.2) | async-done | bytes 524320 | tf_op jit(solution)/shard_map/all_to_all | solution.py:150
  273.0 10.2 %all-to-all-start.1 = ((bf16[32,40,1024]{2,1,0:T(8,128)(2,1)}), bf16[32,40,1024]{2,1,0:T(8,128)(2,1)}, u32[]{:S(2)}, u32[]{:S(2)}) async-start(bf16[32,40,1024]{2,1,0:T(8,128)(2,1)} %bitcast.130), calls=%async_computation.1 | async-start | bytes 5242880 | tf_op jit(solution)/shard_map/all_to_all | solution.py:130
  283.3 0.9 copy.53
  284.1 60.0 %all-to-all-done.1 = bf16[32,40,1024]{2,1,0:T(8,128)(2,1)} async-done(((bf16[32,40,1024]{2,1,0:T(8,128)(2,1)}), bf16[32,40,1024]{2,1,0:T(8,128)(2,1)}, u32[]{:S(2)}, u32[]{:S(2)}) %all-to-all-start.1) | async-done | bytes 2621472 | tf_op jit(solution)/shard_map/all_to_all | solution.py:130
  344.2 8.1 %gather_fusion = bf16[1024,1024]{1,0:T(8,128)(2,1)} fusion(bf16[1280,1024]{1,0:T(8,128)(2,1)} %bitcast.36, s32[1024]{0:T(1024)S(1)} %broadcast_clamp_fusion), kind=kCustom, calls=%fused_computation | custom fusion | bytes 4198400 | tf_op jit(solution)/shard_map/gather | solution.py:132
  352.3 2.9 fusion.5
  356.0 0.8 copy.66
  (63 shorter events, 7.4 us)
Async XLA Ops:
  7.2 252.6 %copy-start = (bf16[1,1024,1024]{2,1,0:T(8,128)(2,1)S(1)}, bf16[1,1024,1024]{2,1,0:T(8,128)(2,1)}, u32[]{:S(2)}) copy-start(bf16[1,1024,1024]{2,1,0:T(8,128)(2,1)} %param.23) | copy-start | bytes 6291460
  7.2 73.0 %all-gather.3.cloned.1.call-start = ((), (), s32[]{:S(2)}) async-start(), calls=%async_computation.3 | async-start | bytes 2228224 | tf_op jit(solution)/shard_map/all_gather | solution.py:88
  7.9 169.3 %all-gather.5.cloned.1.call-start = ((), (), s32[]{:S(2)}) async-start(), calls=%async_computation.4 | async-start | bytes 2162688 | tf_op jit(solution)/shard_map/all_gather | solution.py:100
  85.7 3.0 copy-start.5
  85.7 3.0 copy-start.1
  85.7 3.2 copy-start.7
  88.9 2.2 copy-start.2
  92.7 84.5 %copy-start.4 = (bf16[1,128,1024]{2,1,0:T(8,128)(2,1)S(1)}, bf16[1,128,1024]{2,1,0:T(8,128)(2,1)}, u32[]{:S(2)}) copy-start(bf16[1,128,1024]{2,1,0:T(8,128)(2,1)} %param.13) | copy-start | bytes 786436
  93.0 86.4 %copy-start.6 = (s32[1024,1]{0,1:T(1,128)S(1)}, s32[1024,1]{0,1:T(1,128)}, u32[]{:S(2)}) copy-start(s32[1024,1]{0,1:T(1,128)} %compare_select_fusion) | copy-start | bytes 12292
  186.6 4.8 %copy-start.9 = (s32[1,8,1]{1,2,0:T(1,128)S(1)}, s32[1,8,1]{1,2,0:T(1,128)}, u32[]{:S(2)}) copy-start(s32[1,8,1]{1,2,0:T(1,128)} %param.25) | copy-start | bytes 100
  186.6 5.9 %copy-start.3 = (bf16[1,64,1024]{2,1,0:T(8,128)(2,1)S(1)}, bf16[1,64,1024]{2,1,0:T(8,128)(2,1)}, u32[]{:S(2)}) copy-start(bf16[1,64,1024]{2,1,0:T(8,128)(2,1)} %param.16) | copy-start | bytes 393220
  186.6 65.8 %all-to-all-start = ((bf16[32,40,1024]{2,1,0:T(8,128)(2,1)}), bf16[32,40,1024]{2,1,0:T(8,128)(2,1)}, u32[]{:S(2)}, u32[]{:S(2)}) async-start(bf16[32,40,1024]{2,1,0:T(8,128)(2,1)} %bitcast.128), calls=%async_computation | async-start | bytes 5242880 | tf_op jit(solution)/shard_map/all_to_all | solution.py:119
  252.4 20.6 %all-to-all-start.2 = ((bf16[32,8,1024]{2,1,0:T(8,128)(2,1)}), bf16[32,8,1024]{2,1,0:T(8,128)(2,1)S(1)}, u32[]{:S(2)}, u32[]{:S(2)}) async-start(bf16[32,8,1024]{2,1,0:T(8,128)(2,1)} %scatter_fusion), calls=%async_computation.2 | async-start | bytes 1048576 | tf_op jit(solution)/shard_map/all_to_all | solution.py:150
  259.8 4.8 %copy-start.10 = (bf16[1,512,1024]{2,1,0:T(8,128)(2,1)S(1)}, bf16[1,512,1024]{2,1,0:T(8,128)(2,1)}, u32[]{:S(2)}) copy-start(bf16[1,512,1024]{2,1,0:T(8,128)(2,1)} %param.24) | copy-start | bytes 3145732
  273.0 10.2 %copy-start.8 = (f32[1,128,8]{1,2,0:T(8,128)S(1)}, f32[1,128,8]{1,2,0:T(8,128)}, u32[]{:S(2)}) copy-start(f32[1,128,8]{1,2,0:T(8,128)} %param.22) | copy-start | bytes 12292
  273.0 71.2 %all-to-all-start.1 = ((bf16[32,40,1024]{2,1,0:T(8,128)(2,1)}), bf16[32,40,1024]{2,1,0:T(8,128)(2,1)}, u32[]{:S(2)}, u32[]{:S(2)}) async-start(bf16[32,40,1024]{2,1,0:T(8,128)(2,1)} %bitcast.130), calls=%async_computation.1 | async-start | bytes 5242880 | tf_op jit(solution)/shard_map/all_to_all | solution.py:130
Sparse Core Ops, SparseCore 0:
  10.1 70.0 all-gather.2
  83.6 93.5 all-gather.4
where the time goes:
time: 364 us
  waiting for transfers between devices  244 us (67%)
  local copies, waits for them, and re-layouts  30.7 us (8%)
  starting transfers between devices  22.4 us (6%)
  other arithmetic  19.4 us (5%)
  matrix products  16.7 us (5%)
  between operations  15.7 us (4%)
  blocking collectives  15.1 us (4%)
    all_gather x1, waiting for transfers between devices, local(): lax.all_gather(out_weight, 'exp', axis=0, tiled=True)  84.1 us
    all_to_all x1, waiting for transfers between devices, local(): lax.all_to_all(outgoing, 'exp', split_axis=0, concat_axis=0, tiled=True)  60 us
    all_to_all x1, waiting for transfers between devices, local(): lax.all_to_all(dispatch, 'exp', split_axis=0, concat_axis=0, tiled=True)  57.8 us
    all_gather x1, waiting for transfers between devices, local(): piece_kv = lax.all_gather(prompt_kv, 'blk', axis=1, tiled=True)  35 us
    unnamed x1, blocking collectives  15.1 us
    all_to_all x1, starting transfers between devices, local(): lax.all_to_all(outgoing, 'exp', split_axis=0, concat_axis=0, tiled=True)  10.2 us
    another operation x4, other arithmetic  9.95 us
    gather x1, local copies, waits for them, and re-layouts, local(): returned.reshape(experts * capacity, D)[slot_index].astype(jnp.float32)  8.11 us
  transfers between devices with their start and end apart: 5, of which 5 were waited for; matrix products, arithmetic and copies ran while one was open for 12% of the time, Pallas kernels for 0%

commit v1 on v0

--- a/solution.py
+++ b/solution.py
@@ -15,6 +15,13 @@
 SCALE = 0.125
 NEGATIVE = -1e30
 EPSILON = 1e-06
+
+
+def write_panels_all(on_dim, mine):
+    return jnp.concatenate(
+        lax.all_to_all(jnp.stack(tuple((mine for _ in range(lax.axis_size("exp"))))), "exp", 0, 0),
+        axis=on_dim,
+    )
 
 
 def segment_of(lengths, count):
@@ -96,9 +103,7 @@
     )
     attended = (numerator / denom[..., None]).reshape(tok_rows, H * HD).astype(jnp.bfloat16)
     projected = jnp.dot(
-        attended,
-        lax.all_gather(out_weight, "exp", axis=0, tiled=True),
-        preferred_element_type=jnp.float32,
+        attended, write_panels_all(0, out_weight), preferred_element_type=jnp.float32
     )
     stream = (residual[0].astype(jnp.float32) + projected).astype(jnp.bfloat16)
     stream_f32 = stream.astype(jnp.float32)

time: 364 us -> 295 us (0.81)
  waiting for transfers between devices: 244 us -> 150 us
  starting transfers between devices: 22.4 us -> 48.1 us
    all_gather x1 -> x0, waiting for transfers between devices: 84.1 us -> none  [local(): lax.all_gather(out_weight, 'exp', axis=0, tiled=True)]
    all_to_all x1, starting transfers between devices: 4.77 us -> 19.4 us  [local(): lax.all_to_all(dispatch, 'exp', split_axis=0, concat_axis=0, tiled=True)]
    all_to_all x0 -> x1, starting transfers between devices: none -> 14.6 us  [write_panels_all(): lax.all_to_all(jnp.stack(tuple((mine for _ in range(lax.axis_size('exp'))...]
    all_gather x1, waiting for transfers between devices: 35 us -> 26.5 us  [local(): piece_kv = lax.all_gather(prompt_kv, 'blk', axis=1, tiled=True)]
  transfers between devices with their start and end apart: 5 -> 5, of which waited for: 5 -> 4; matrix products, arithmetic and copies ran while one was open for 12% -> 15% of each run, Pallas kernels for 0% -> 0%
where the time goes in v1:
time: 295 us; the launch traced here: 294 us
  waiting for transfers between devices  150 us (51%)
  starting transfers between devices  48.1 us (16%)
  local copies, waits for them, and re-layouts  32 us (11%)
  other arithmetic  17.4 us (6%)
  matrix products  16.8 us (6%)
  between operations  15.7 us (5%)
  blocking collectives  14 us (5%)
    all_to_all x1, waiting for transfers between devices, local(): lax.all_to_all(outgoing, 'exp', split_axis=0, concat_axis=0, tiled=True)  60 us
    all_to_all x1, waiting for transfers between devices, local(): lax.all_to_all(dispatch, 'exp', split_axis=0, concat_axis=0, tiled=True)  57.8 us
    all_gather x1, waiting for transfers between devices, local(): piece_kv = lax.all_gather(prompt_kv, 'blk', axis=1, tiled=True)  26.5 us
    all_to_all x1, starting transfers between devices, local(): lax.all_to_all(dispatch, 'exp', split_axis=0, concat_axis=0, tiled=True)  19.4 us
    all_to_all x1, starting transfers between devices, write_panels_all(): lax.all_to_all(jnp.stack(tuple((mine for _ in range(lax.axis_size('exp'))...  14.6 us
    unnamed x1, blocking collectives  14 us
    all_to_all x1, starting transfers between devices, local(): lax.all_to_all(outgoing, 'exp', split_axis=0, concat_axis=0, tiled=True)  10.1 us
    another operation x4, other arithmetic  9.32 us
  transfers between devices with their start and end apart: 5, of which 4 were waited for; matrix products, arithmetic and copies ran while one was open for 15% of the time, Pallas kernels for 0%

profile of v1, /device:TPU:1, one launch (start us, length us, event | category | flops | bytes accessed | tf_op | source)
XLA Modules:
  0.0 294.4 jit_solution(14720587101093367091)
XLA Ops:
  7.2 0.7 all-gather.2.cloned.1.call-update
  7.9 2.4 stack.2
  10.3 14.6 %all-to-all-start = ((bf16[32,32,1024]{2,1,0:T(8,128)(2,1)}), bf16[32,32,1024]{2,1,0:T(8,128)(2,1)}, u32[]{:S(2)}, u32[]{:S(2)}) async-start(bf16[32,32,1024]{2,1,0:T(8,128)(2,1)} %stack.2), calls=%async_computation | async-start | bytes 4194304 | tf_op jit(solution)/shard_map/all_to_all | solution.py:22
  26.2 9.0 %reduce-window.19 = s32[32,8,128]{2,1,0:T(8,128)S(1)} reduce-window(s32[32,8,128]{2,1,0:T(8,128)S(1)} %fusion.39, s32[]{:T(128)} %constant.17.clone.1), window={size=1x1x128 pad=0_0x0_0x127_0}, to_apply=%region_6.7 | reduce-window | flops 4161536 | bytes 262148 | tf_op jit(solution)/shard_map/reduce-window.1
  35.6 1.3 dynamic-slice
  38.0 1.1 copy.41
  39.5 14.0 %all-reduce = s32[1024]{0:T(1024)S(1)} all-reduce(s32[1024]{0:T(1024)S(1)} %fusion.43), channel_id=1, replica_groups=mesh['blk'=16,'exp'=32] {'blk'}, use_global_device_ids=true, to_apply=%add | all-reduce | flops 1024 | bytes 8192
  54.9 2.0 select_reduce_fusion
  56.8 26.5 %all-gather.2.cloned.1.call-done = bf16[1,1024,1024]{2,1,0:T(8,128)(2,1)} async-done(((bf16[1,64,1024]{2,1,0:T(8,128)(2,1)}), bf16[1,1024,1024]{2,1,0:T(8,128)(2,1)}) %all-gather.2.cloned.1.call-update) | async-done | bytes 2097168 | tf_op jit(solution)/shard_map/all_gather | solution.py:95
  83.4 2.7 fusion.50
  86.0 1.3 copy.45
  87.4 1.5 copy.44
  88.9 2.9 %fusion = (f32[128,8,2]{0,2,1:T(2,128)S(1)}, f32[8,1024,128,2]{2,1,3,0:T(8,128)S(1)}) fusion(pred[1024]{0:T(1024)(128)(4,1)} %broadcast_compare_fusion, bf16[1024,8,64,1]{0,2,3,1:T(8,128)(2,1)S(1)} %bitcast.130, bf16[128,8,2,64]{0,3,2,1:T(8,128)(2,1)S(1)} %bitcast.133), kind=kOutput, calls=%fused_computation.5 | convolution fusion | flops 274724864 | bytes 9708544 | tf_op jit(solution)/shard_map/tkgd,skd->tkgs/dot_general | solution.py:42
  92.1 2.2 fusion.3
  94.3 1.5 fusion.17
  96.8 2.1 multiply_reduce_fusion
  99.1 7.1 %scatter_custom_fusion = bf16[1280,1024]{1,0:T(8,128)(2,1)} fusion(s32[1024]{0:T(1024)S(1)} %bitcast.144, bf16[]{:T(256)} %constant.12.clone.1, bf16[128,1024]{1,0:T(8,128)(2,1)S(1)} %multiply_convert_fusion), kind=kCustom, calls=%fused_computation.19 | custom fusion | bytes 2883586 | tf_op jit(solution)/shard_map/scatter | solution.py:121
  106.2 19.4 %all-to-all-start.1 = ((bf16[32,40,1024]{2,1,0:T(8,128)(2,1)}), bf16[32,40,1024]{2,1,0:T(8,128)(2,1)}, u32[]{:S(2)}, u32[]{:S(2)}) async-start(bf16[32,40,1024]{2,1,0:T(8,128)(2,1)} %bitcast.129), calls=%async_computation.1 | async-start | bytes 5242880 | tf_op jit(solution)/shard_map/all_to_all | solution.py:124
  125.9 0.9 broadcast_in_dim.91
  126.8 2.1 scatter_fusion
  128.9 57.8 %all-to-all-done.1 = bf16[32,40,1024]{2,1,0:T(8,128)(2,1)} async-done(((bf16[32,40,1024]{2,1,0:T(8,128)(2,1)}), bf16[32,40,1024]{2,1,0:T(8,128)(2,1)}, u32[]{:S(2)}, u32[]{:S(2)}) %all-to-all-start.1) | async-done | bytes 2621472 | tf_op jit(solution)/shard_map/all_to_all | solution.py:124
  186.7 3.9 %all-to-all-start.3 = ((bf16[32,8,1024]{2,1,0:T(8,128)(2,1)}), bf16[32,8,1024]{2,1,0:T(8,128)(2,1)S(1)}, u32[]{:S(2)}, u32[]{:S(2)}) async-start(bf16[32,8,1024]{2,1,0:T(8,128)(2,1)} %scatter_fusion), calls=%async_computation.3 | async-start | bytes 1048576 | tf_op jit(solution)/shard_map/all_to_all | solution.py:155
  190.6 4.7 %fusion.10 = f32[1280,1024]{1,0:T(8,128)S(1)} fusion(bf16[1280,1024]{1,0:T(8,128)(2,1)} %bitcast.33, bf16[1,1024,1024]{2,1,0:T(8,128)(2,1)S(1)} %copy-done), kind=kOutput, calls=%fused_computation.17 | convolution fusion | flops 2684354560 | bytes 9961472 | tf_op jit(solution)/shard_map/dot_general | solution.py:128
  195.4 3.1 %convolution_convert_fusion = bf16[1280,1024]{1,0:T(8,128)(2,1)} fusion(f32[1280,1024]{1,0:T(8,128)S(1)} %fusion.10, bf16[1,512,1024]{2,1,0:T(8,128)(2,1)S(1)} %copy-done.12), kind=kOutput, calls=%fused_computation.14 | convolution fusion | flops 1347420160 | bytes 8912896 | tf_op jit(solution)/shard_map/dot_general | solution.py:130
  198.5 5.3 %all-to-all-done.3 = bf16[32,8,1024]{2,1,0:T(8,128)(2,1)S(1)} async-done(((bf16[32,8,1024]{2,1,0:T(8,128)(2,1)}), bf16[32,8,1024]{2,1,0:T(8,128)(2,1)S(1)}, u32[]{:S(2)}, u32[]{:S(2)}) %all-to-all-start.3) | async-done | bytes 524320 | tf_op jit(solution)/shard_map/all_to_all | solution.py:155
  203.8 10.1 %all-to-all-start.2 = ((bf16[32,40,1024]{2,1,0:T(8,128)(2,1)}), bf16[32,40,1024]{2,1,0:T(8,128)(2,1)}, u32[]{:S(2)}, u32[]{:S(2)}) async-start(bf16[32,40,1024]{2,1,0:T(8,128)(2,1)} %bitcast.131), calls=%async_computation.2 | async-start | bytes 5242880 | tf_op jit(solution)/shard_map/all_to_all | solution.py:135
  214.0 0.9 copy.53
  214.9 60.0 %all-to-all-done.2 = bf16[32,40,1024]{2,1,0:T(8,128)(2,1)} async-done(((bf16[32,40,1024]{2,1,0:T(8,128)(2,1)}), bf16[32,40,1024]{2,1,0:T(8,128)(2,1)}, u32[]{:S(2)}, u32[]{:S(2)}) %all-to-all-start.2) | async-done | bytes 2621472 | tf_op jit(solution)/shard_map/all_to_all | solution.py:135
  274.9 8.1 %gather_fusion = bf16[1024,1024]{1,0:T(8,128)(2,1)} fusion(bf16[1280,1024]{1,0:T(8,128)(2,1)} %bitcast.37, s32[1024]{0:T(1024)S(1)} %broadcast_clamp_fusion), kind=kCustom, calls=%fused_computation | custom fusion | bytes 4198400 | tf_op jit(solution)/shard_map/gather | solution.py:137
  283.0 2.9 fusion.5
  286.0 0.8 fusion.35
  286.7 0.8 copy.66
  (71 shorter events, 4.8 us)
Async XLA Ops:
  7.2 183.4 %copy-start = (bf16[1,1024,1024]{2,1,0:T(8,128)(2,1)S(1)}, bf16[1,1024,1024]{2,1,0:T(8,128)(2,1)}, u32[]{:S(2)}) copy-start(bf16[1,1024,1024]{2,1,0:T(8,128)(2,1)} %param.23) | copy-start | bytes 6291460
  7.2 76.2 %all-gather.2.cloned.1.call-start = ((), (), s32[]{:S(2)}) async-start(), calls=%async_computation.4 | async-start | bytes 2228224 | tf_op jit(solution)/shard_map/all_gather | solution.py:95
  10.3 14.7 %copy-start.13 = (s32[1,2]{1,0:T(1,128)S(1)}, s32[1,2]{1,0:T(1,128)}, u32[]{:S(2)}) copy-start(s32[1,2]{1,0:T(1,128)} %param.18) | copy-start | bytes 28
  10.3 15.5 %copy-start.7 = (s32[1,128,8]{1,2,0:T(8,128)S(1)}, s32[1,128,8]{1,2,0:T(8,128)}, u32[]{:S(2)}) copy-start(s32[1,128,8]{1,2,0:T(8,128)} %param.21) | copy-start | bytes 12292
  10.3 15.7 %copy-start.14 = (s32[1,1,4]{2,1,0:T(1,128)S(1)}, s32[1,1,4]{2,1,0:T(1,128)}, u32[]{:S(2)}) copy-start(s32[1,1,4]{2,1,0:T(1,128)} %param.19) | copy-start | bytes 52
  10.3 27.4 %copy-start.4 = (bf16[1,128,1024]{2,1,0:T(8,128)(2,1)S(1)}, bf16[1,128,1024]{2,1,0:T(8,128)(2,1)}, u32[]{:S(2)}) copy-start(bf16[1,128,1024]{2,1,0:T(8,128)(2,1)} %param.15) | copy-start | bytes 786436
  10.3 85.9 %all-to-all-start = ((bf16[32,32,1024]{2,1,0:T(8,128)(2,1)}), bf16[32,32,1024]{2,1,0:T(8,128)(2,1)}, u32[]{:S(2)}, u32[]{:S(2)}) async-start(bf16[32,32,1024]{2,1,0:T(8,128)(2,1)} %stack.2), calls=%async_computation | async-start | bytes 4194304 | tf_op jit(solution)/shard_map/all_to_all | solution.py:22
  88.8 3.0 %copy-start.6 = (f32[128,8,2]{0,2,1:T(2,128)S(1)}, f32[128,8,2]{0,2,1:T(2,128)}, u32[]{:S(2)}) copy-start(f32[128,8,2]{0,2,1:T(2,128)} %get-tuple-element.21) | copy-start | bytes 24580
  88.9 3.0 %copy-start.1 = (f32[128,8,2,128]{0,3,2,1:T(8,128)S(1)}, f32[128,8,2,128]{0,3,2,1:T(8,128)}, u32[]{:S(2)}) copy-start(f32[128,8,2,128]{0,3,2,1:T(8,128)} %get-tuple-element.22) | copy-start | bytes 3145732
  88.9 3.2 %copy-start.9 = (pred[1024]{0:T(1024)(128)(4,1)S(1)}, pred[1024]{0:T(1024)(128)(4,1)}, u32[]{:S(2)}) copy-start(pred[1024]{0:T(1024)(128)(4,1)} %broadcast_compare_fusion) | copy-start | bytes 3076
  92.1 2.2 copy-start.2
  95.9 1.0 copy-start.5
  96.2 2.9 copy-start.8
  106.2 19.4 %copy-start.11 = (s32[1,8,1]{1,2,0:T(1,128)S(1)}, s32[1,8,1]{1,2,0:T(1,128)}, u32[]{:S(2)}) copy-start(s32[1,8,1]{1,2,0:T(1,128)} %param.25) | copy-start | bytes 100
  106.2 20.6 %copy-start.3 = (bf16[1,64,1024]{2,1,0:T(8,128)(2,1)S(1)}, bf16[1,64,1024]{2,1,0:T(8,128)(2,1)}, u32[]{:S(2)}) copy-start(bf16[1,64,1024]{2,1,0:T(8,128)(2,1)} %param.16) | copy-start | bytes 393220
  106.2 80.4 %all-to-all-start.1 = ((bf16[32,40,1024]{2,1,0:T(8,128)(2,1)}), bf16[32,40,1024]{2,1,0:T(8,128)(2,1)}, u32[]{:S(2)}, u32[]{:S(2)}) async-start(bf16[32,40,1024]{2,1,0:T(8,128)(2,1)} %bitcast.129), calls=%async_computation.1 | async-start | bytes 5242880 | tf_op jit(solution)/shard_map/all_to_all | solution.py:124
  186.7 17.1 %all-to-all-start.3 = ((bf16[32,8,1024]{2,1,0:T(8,128)(2,1)}), bf16[32,8,1024]{2,1,0:T(8,128)(2,1)S(1)}, u32[]{:S(2)}, u32[]{:S(2)}) async-start(bf16[32,8,1024]{2,1,0:T(8,128)(2,1)} %scatter_fusion), calls=%async_computation.3 | async-start | bytes 1048576 | tf_op jit(solution)/shard_map/all_to_all | solution.py:155
  190.6 4.8 %copy-start.12 = (bf16[1,512,1024]{2,1,0:T(8,128)(2,1)S(1)}, bf16[1,512,1024]{2,1,0:T(8,128)(2,1)}, u32[]{:S(2)}) copy-start(bf16[1,512,1024]{2,1,0:T(8,128)(2,1)} %param.24) | copy-start | bytes 3145732
  203.8 10.1 %copy-start.10 = (f32[1,128,8]{1,2,0:T(8,128)S(1)}, f32[1,128,8]{1,2,0:T(8,128)}, u32[]{:S(2)}) copy-start(f32[1,128,8]{1,2,0:T(8,128)} %param.22) | copy-start | bytes 12292
  203.8 71.1 %all-to-all-start.2 = ((bf16[32,40,1024]{2,1,0:T(8,128)(2,1)}), bf16[32,40,1024]{2,1,0:T(8,128)(2,1)}, u32[]{:S(2)}, u32[]{:S(2)}) async-start(bf16[32,40,1024]{2,1,0:T(8,128)(2,1)} %bitcast.131), calls=%async_computation.2 | async-start | bytes 5242880 | tf_op jit(solution)/shard_map/all_to_all | solution.py:135
Sparse Core Ops, SparseCore 0:
  10.1 73.2 all-gather.1
